TPU v7x, 256 devices: a whole 4x4x8 slice. The times are simulated.
256 devices in a mesh: req: 8 (over z), exp: 8 (over y, core), hid: 4 (over x).
Axes of the slice: x: 4, y: 4, z: 8, core: 2. Of those that a mesh axis runs over, the one named last changes fastest.
Arguments:
- layer_input_rows: bfloat16 [16384, 1536], P(('req', 'exp')), may hold values from -6 to 6
- attention_norm_gain: float32 [1536], replicated
- query_weight: bfloat16 [1536, 1536], P(None, 'hid'), may hold values from -1 to 1
- key_weight: bfloat16 [1536, 512], P(None, 'hid'), may hold values from -1 to 1
- value_weight: bfloat16 [1536, 512], P(None, 'hid'), may hold values from -0.15625 to 0.15625
- attention_output_weight: bfloat16 [1536, 1536], P('hid'), may hold values from -0.15625 to 0.15625
- query_down_factor: bfloat16 [64, 1536, 16], P(('req', 'exp')), may hold values from -0.15625 to 0.15625
- query_up_factor: bfloat16 [64, 16, 1536], P(('req', 'exp')), may hold values from -1.5 to 1.5
- value_down_factor: bfloat16 [64, 1536, 16], P(('req', 'exp')), may hold values from -0.15625 to 0.15625
- value_up_factor: bfloat16 [64, 16, 512], P(('req', 'exp')), may hold values from -1.5 to 1.5
- lengths: int32 [8, 4], P('req'), may hold values from 1 to 1024, 2048 in all within a row
- request_adapter: int32 [8, 4], replicated, may hold values from 0 to 63
- adapter_home_row: int32 [64], replicated, may hold values from 0 to 63, each once
- expert_norm_gain: float32 [1536], replicated, may hold values from 0.4 to 1.6
- routes: int32 [16384, 8], P(('req', 'exp', 'hid')), may hold values from 0 to 39, all different within a row; in each aligned block of 64 rows (0 to 63, 64 to 127, ...) at most 16 rows name the same one
- router_expert_weight: float32 [16384, 8], P(('req', 'exp', 'hid')), may hold values from 0.1 to 0.5
- expert_gate_weight: bfloat16 [40, 1536, 512], P('exp', None, 'hid'), may hold values from -0.15625 to 0.15625
- expert_up_weight: bfloat16 [40, 1536, 512], P('exp', None, 'hid'), may hold values from -0.15625 to 0.15625
- expert_down_weight: bfloat16 [40, 512, 1536], P('exp', 'hid'), may hold values from -0.25 to 0.25
Outputs:
- attn_out: bfloat16 [16384, 1536], P(('req', 'exp', 'hid'))
- expert_out: bfloat16 [16384, 1536], P(('req', 'exp', 'hid'))
Inputs may be any that keep to these rules, and one draw needn't show every extreme that they name: `lengths`: each row sums to 2048; its largest entry is exactly 1024. `adapter_home_row`: each adapter row appears once. `routes`: A row names 8 different experts. In the rows of one device (64 consecutive rows, aligned) no expert is named more than 16 times, a bound that some block reaches in some of them.
All inputs are finite; a program needn't handle non-finite values.
Results may differ from a plain program's by a relative error of at most 0.029.
The roundings to bfloat16 on the way count: a program that leaves them out, or rounds other values in their place, can miss the bound.
Values may be sent and summed in bfloat16 or wider, within the bound.
No kernel may reach another device: no remote copies, remote signals or barrier semaphores. Data moves between devices by JAX's collectives and lax.ppermute only.
A program may use at most 128 MiB of HBM per device.

v0:
```python
import jax
import jax.numpy as jnp
from jax import lax
from jax.sharding import PartitionSpec as P

HEAD_WIDTH = 64
scale_attn = 0.015625
residual_mult = 0.22
norm_eps = 1e-06
rope_base = 10000.0
neg_large = -1e30


def rms_norm(values, norm_gain):
    widened = values.astype(jnp.float32)
    mean_sq = jnp.mean(widened * widened, axis=-1, keepdims=True)
    return (widened * lax.rsqrt(mean_sq + norm_eps) * norm_gain).astype(jnp.bfloat16)


def rotary(heads_in, position):
    half_size = heads_in.shape[-1] // 2
    frequency = rope_base ** (-2.0 * jnp.arange(half_size, dtype=jnp.float32) / heads_in.shape[-1])
    angles = position.astype(jnp.float32)[:, None] * frequency[None, :]
    cosine = jnp.cos(angles)[:, None, :]
    sine_part = jnp.sin(angles)[:, None, :]
    first_half = heads_in[..., :half_size]
    second_half = heads_in[..., half_size:]
    return jnp.concatenate(
        [
            first_half * cosine - second_half * sine_part,
            second_half * cosine + first_half * sine_part,
        ],
        axis=-1,
    )


def request_of(row_ids, group_len):
    request_end = jnp.cumsum(group_len)
    return jnp.sum((row_ids[:, None] >= request_end[None, :]).astype(jnp.int32), axis=1)


def locate(row_ids, group_len):
    request_end = jnp.cumsum(group_len)
    request_start = request_end - group_len
    request = request_of(row_ids, group_len)
    member = request[:, None] == jnp.arange(group_len.shape[0], dtype=jnp.int32)[None, :]
    position = row_ids - jnp.sum(jnp.where(member, request_start[None, :], 0), axis=1)
    return (request, member, position)


def expert_rows(rows_in, expert_gate_weight, expert_up_weight, expert_down_weight):
    gate_act = jnp.einsum(
        "red,edf->ref", rows_in, expert_gate_weight, preferred_element_type=jnp.float32
    )
    upper = jnp.einsum(
        "red,edf->ref", rows_in, expert_up_weight, preferred_element_type=jnp.float32
    )
    hidden = (jax.nn.silu(gate_act) * upper).astype(jnp.bfloat16)
    return jnp.einsum(
        "ref,efd->red", hidden, expert_down_weight, preferred_element_type=jnp.float32
    )


def per_device(
    layer_input_rows,
    attention_norm_gain,
    query_weight,
    key_weight,
    value_weight,
    attention_output_weight,
    query_down_factor,
    query_up_factor,
    value_down_factor,
    value_up_factor,
    lengths,
    request_adapter,
    adapter_home_row,
    expert_norm_gain,
    routes,
    router_expert_weight,
    expert_gate_weight,
    expert_up_weight,
    expert_down_weight,
):
    exp_count = lax.axis_size("exp")
    hid_count = lax.axis_size("hid")
    exp_index = lax.axis_index("exp")
    hid_index = lax.axis_index("hid")
    req_index = lax.axis_index("req")
    query_rows = layer_input_rows.shape[0]
    width = layer_input_rows.shape[1]
    kv_local = key_weight.shape[1] // HEAD_WIDTH
    q_local = query_weight.shape[1] // HEAD_WIDTH
    group_share = q_local // kv_local
    adapter_rank_size = query_down_factor.shape[2]
    requests = lengths.shape[1]
    group_len = lengths[0]
    row_ids = exp_index * query_rows + jnp.arange(query_rows, dtype=jnp.int32)
    request, member, position = locate(row_ids, group_len)
    wanted = lax.dynamic_index_in_dim(request_adapter, req_index, 0, keepdims=False)
    slot_ids = jnp.arange(adapter_home_row.shape[0], dtype=jnp.int32)
    home_of = jnp.sum(
        jnp.where(wanted[:, None] == slot_ids[None, :], adapter_home_row[None, :], 0), axis=1
    )
    query_cols = q_local * HEAD_WIDTH
    kv_cols = kv_local * HEAD_WIDTH
    bank_local = query_down_factor.shape[0]
    up_q = lax.dynamic_slice_in_dim(query_up_factor, hid_index * query_cols, query_cols, 2)
    up_v = lax.dynamic_slice_in_dim(value_up_factor, hid_index * kv_cols, kv_cols, 2)
    parts_in = (query_down_factor, up_q, value_down_factor, up_v)
    part_shapes = [p.shape[1:] for p in parts_in]
    part_sizes = [p.shape[1] * p.shape[2] for p in parts_in]
    bank = jnp.concatenate([p.reshape(bank_local, -1) for p in parts_in], axis=1)
    along_req = lax.all_gather(bank, "req", axis=0, tiled=True)
    home_dev = home_of // bank_local
    home_pick = home_dev // exp_count * bank_local + home_of % bank_local
    mine = home_dev % exp_count == exp_index
    rows_pick = jnp.take(along_req, home_pick, axis=0)
    rows_pick = jnp.where(mine[:, None], rows_pick, jnp.zeros_like(rows_pick))
    rows_pick = lax.psum(rows_pick, "exp")
    chosen = []
    start = 0
    for shape_in, size_in in zip(part_shapes, part_sizes):
        chosen.append(rows_pick[:, start : start + size_in].reshape((requests,) + shape_in))
        start += size_in
    qa_sel, qb_sel, va_sel, vb_sel = chosen
    normed_rows = rms_norm(layer_input_rows, attention_norm_gain)

    def low_rank_term(a_sel, b_sel, width_cols, offset):
        inner_terms = jnp.einsum(
            "td,jdr->tjr", normed_rows, a_sel, preferred_element_type=jnp.float32
        )
        inner_terms = (
            jnp.where(member[:, :, None], inner_terms, 0.0)
            .reshape(query_rows, requests * adapter_rank_size)
            .astype(jnp.bfloat16)
        )
        right_factor = b_sel.reshape(requests * adapter_rank_size, width_cols)
        return jnp.dot(inner_terms, right_factor, preferred_element_type=jnp.float32)

    query_matrix = jnp.dot(
        normed_rows, query_weight, preferred_element_type=jnp.float32
    ) + low_rank_term(qa_sel, qb_sel, query_cols, hid_index * query_cols)
    query_matrix = rotary(query_matrix.reshape(query_rows, q_local, HEAD_WIDTH), position).astype(
        jnp.bfloat16
    )
    query_matrix = query_matrix.reshape(query_rows, kv_local, group_share, HEAD_WIDTH)
    keys_own = jnp.dot(normed_rows, key_weight, preferred_element_type=jnp.float32)
    keys_own = (
        rotary(keys_own.reshape(query_rows, kv_local, HEAD_WIDTH), position)
        .astype(jnp.bfloat16)
        .reshape(query_rows, kv_cols)
    )
    values_own = jnp.dot(
        normed_rows, value_weight, preferred_element_type=jnp.float32
    ) + low_rank_term(va_sel, vb_sel, kv_cols, hid_index * kv_cols)
    values_own = values_own.astype(jnp.bfloat16)
    running_max = jnp.full((kv_local, group_share, query_rows), neg_large, jnp.float32)
    key_piece = lax.all_gather(keys_own, "exp", axis=0, tiled=True)
    value_piece = lax.all_gather(values_own, "exp", axis=0, tiled=True)
    piece_len = key_piece.shape[0]
    key_ids = jnp.arange(piece_len, dtype=jnp.int32)
    key_request = request_of(key_ids, group_len)
    allowed = (request[:, None] == key_request[None, :]) & (key_ids[None, :] <= row_ids[:, None])
    key_heads = key_piece.reshape(piece_len, kv_local, HEAD_WIDTH)
    value_heads = value_piece.reshape(piece_len, kv_local, HEAD_WIDTH)
    scores = (
        jnp.einsum("qkgh,nkh->kgqn", query_matrix, key_heads, preferred_element_type=jnp.float32)
        * scale_attn
    )
    scores = jnp.where(allowed[None, None], scores, neg_large)
    new_max = jnp.maximum(running_max, jnp.max(scores, axis=-1))
    weights = jnp.where(allowed[None, None], jnp.exp(scores - new_max[..., None]), 0.0)
    running_sum = jnp.sum(weights, axis=-1)
    running_out = jnp.einsum(
        "kgqn,nkh->kgqh",
        weights.astype(jnp.bfloat16),
        value_heads,
        preferred_element_type=jnp.float32,
    )
    running_max, running_sum, running_out = (new_max, running_sum, running_out)
    attended = (running_out / running_sum[..., None]).astype(jnp.bfloat16)
    attended = jnp.transpose(attended, (2, 0, 1, 3)).reshape(query_rows, query_cols)
    tok_rows = query_rows // hid_count
    attn_out = lax.psum_scatter(
        jnp.dot(attended, attention_output_weight, preferred_element_type=jnp.float32).astype(
            jnp.bfloat16
        ),
        "hid",
        scatter_dimension=0,
        tiled=True,
    )
    own_rows = lax.dynamic_slice_in_dim(layer_input_rows, hid_index * tok_rows, tok_rows, 0)
    mixed_rows = own_rows.astype(jnp.float32) + residual_mult * attn_out.astype(jnp.float32)
    normed_moe = rms_norm(mixed_rows, expert_norm_gain)
    local_exp = expert_gate_weight.shape[0]
    expert_count = local_exp * exp_count
    top_count = routes.shape[1]
    capacity = max(2, tok_rows // 4)
    flat_route = routes.reshape(tok_rows * top_count)
    route_hits = (flat_route[:, None] == jnp.arange(expert_count, dtype=jnp.int32)[None, :]).astype(
        jnp.int32
    )
    earlier = jnp.cumsum(route_hits, axis=0) - route_hits
    slot_pos = jnp.sum(earlier * route_hits, axis=1)
    slots = slot_pos * expert_count + flat_route
    slot_table = jnp.arange(capacity * expert_count, dtype=jnp.int32)
    placed = jnp.any(
        slot_table[:, None, None] == slots.reshape(tok_rows, top_count)[None], axis=2
    ).astype(jnp.bfloat16)
    outgoing = jnp.dot(placed, normed_moe, preferred_element_type=jnp.float32).astype(jnp.bfloat16)
    outgoing = outgoing.reshape(capacity, expert_count, width)
    copies = jnp.broadcast_to(
        outgoing.reshape(capacity, exp_count, 1, local_exp, width),
        (capacity, exp_count, hid_count, local_exp, width),
    )
    copies = copies.reshape(capacity, exp_count * hid_count * local_exp, width)
    arrived = lax.all_to_all(copies, ("exp", "hid"), split_axis=1, concat_axis=0, tiled=True)
    partials = expert_rows(
        arrived, expert_gate_weight, expert_up_weight, expert_down_weight
    ).astype(jnp.bfloat16)
    returned = lax.all_to_all(partials, ("exp", "hid"), split_axis=0, concat_axis=1, tiled=True)
    returned = returned.reshape(capacity, exp_count, hid_count, local_exp, width)
    results = jnp.sum(returned.astype(jnp.float32), axis=2).astype(jnp.bfloat16)
    results = results.reshape(capacity * expert_count, width)
    picked = jnp.take(results, slots, axis=0).reshape(tok_rows, top_count, width)
    expert_out = jnp.sum(
        router_expert_weight[:, :, None] * picked.astype(jnp.float32), axis=1
    ).astype(jnp.bfloat16)
    return (attn_out, expert_out)


def solution(mesh):
    in_specs = (
        P(("req", "exp"), None),
        P(),
        P(None, "hid"),
        P(None, "hid"),
        P(None, "hid"),
        P("hid", None),
        P(("req", "exp"), None, None),
        P(("req", "exp"), None, None),
        P(("req", "exp"), None, None),
        P(("req", "exp"), None, None),
        P("req", None),
        P(),
        P(),
        P(),
        P(("req", "exp", "hid"), None),
        P(("req", "exp", "hid"), None),
        P("exp", None, "hid"),
        P("exp", None, "hid"),
        P("exp", "hid", None),
    )
    out_specs = (P(("req", "exp", "hid"), None), P(("req", "exp", "hid"), None))
    return jax.shard_map(
        per_device, mesh=mesh, in_specs=in_specs, out_specs=out_specs, check_vma=False
    )
```

profile of v0, /device:TPU:1, one launch (start us, length us, event | category | flops | bytes accessed | tf_op | source)
XLA Modules:
  0.0 535.5 jit_solution(14082683978876960325)
XLA Ops:
  11.7 29.4 %all-gather = bf16[8,1,57344]{2,1,0:T(2,128)(2,1)S(1)} all-gather(bf16[1,1,57344]{2,1,0:T(2,128)(2,1)S(1)} %maximum_bitcast_fusion), channel_id=1, replica_groups=mesh['req'=8,'exp'=8,'hid'=4] {'req'}, dimensions={0}, use_global_device_ids=true | all-gather | bytes 1032192 | tf_op jit(solution)/shard_map/all_gather | solution.py:114
  44.7 1.4 fusion.7
  46.6 2.6 fusion.56
  51.8 19.2 %all_gather.9 = bf16[2048,128]{0,1:T(8,128)(2,1)} all-gather(bf16[256,128]{0,1:T(8,128)(2,1)S(1)} %bitcast.160), channel_id=1, replica_groups=mesh['req'=8,'exp'=8,'hid'=4] {'exp'}, dimensions={0}, use_global_device_ids=true | all-gather | bytes 589824 | tf_op jit(solution)/shard_map/all_gather | solution.py:159
  71.1 41.2 %all-reduce.2.cloned.1.call-done = bf16[4,57344]{1,0:T(4,128)(2,1)} async-done(((bf16[4,57344]{1,0:T(4,128)(2,1)}), bf16[4,57344]{1,0:T(4,128)(2,1)}) %all-reduce.2.cloned.1.call-update) | async-done | bytes 458768 | tf_op jit(solution)/shard_map/psum | solution.py:120
  112.3 1.9 fusion.60
  114.2 2.1 reshape.381
  117.5 2.2 fusion.54
  119.7 2.1 reshape.383
  123.1 1.7 fusion.51
  127.1 7.7 %fusion = (f32[2,3,256]{2,1,0:T(4,128)S(1)}, f32[2,2048,256,3]{2,1,3,0:T(8,128)}) fusion(pred[256,2048]{0,1:T(8,128)(4,1)S(1)} %copy-done.2, bf16[2048,2,64,1]{0,2,3,1:T(8,128)(2,1)} %bitcast.158, bf16[256,2,3,32]{0,3,2,1:T(8,128)(2,1)S(1)} %bitcast.169, bf16[256,2,3,32]{0,3,2,1:T(8,128)(2,1)S(1)} %bitcast.168), kind=kOutput, calls=%fused_computation.4 | convolution fusion | flops 412482048 | bytes 13834240 | tf_op jit(solution)/shard_map/qkgh,nkh->kgqn/dot_general | solution.py:168
  135.0 1.4 fusion.21
  136.5 15.9 %all_gather.11 = bf16[2048,128]{1,0:T(8,128)(2,1)S(1)} all-gather(bf16[256,128]{1,0:T(8,128)(2,1)S(1)} %fusion.21), channel_id=1, replica_groups=mesh['req'=8,'exp'=8,'hid'=4] {'exp'}, dimensions={0}, use_global_device_ids=true | all-gather | bytes 589824 | tf_op jit(solution)/shard_map/all_gather | solution.py:160
  152.6 6.9 %fusion.1 = f32[2,3,256]{2,1,0:T(4,128)S(1)} fusion(f32[2,2048,256,3]{2,1,3,0:T(8,128)} %get-tuple-element.17, f32[2,3,256]{2,1,0:T(4,128)S(1)} %broadcast_maximum_fusion, pred[256,2048]{0,1:T(8,128)(4,1)S(1)} %copy-done.2), kind=kLoop, calls=%fused_computation.5 | loop fusion | flops 15727104 | bytes 13119488 | tf_op jit(solution)/shard_map/reduce_sum | solution.py:174
  160.8 3.6 fusion.25
  164.5 1.5 convolution_convert_fusion.1
  168.6 19.8 %reduce-scatter.2.cloned.1.call-done = bf16[64,1536]{1,0:T(8,128)(2,1)} async-done(((bf16[256,1536]{1,0:T(8,128)(2,1)}), bf16[64,1536]{1,0:T(8,128)(2,1)}) %reduce-scatter.2.cloned.1.call-update) | async-done | bytes 196624 | tf_op jit(solution)/shard_map/reduce_scatter | solution.py:185
  189.5 3.0 convolution_convert_fusion
  192.5 4.3 broadcast_in_dim.153
  196.7 3.2 copy.113
  200.9 98.1 %all_to_all.33 = bf16[16,160,1536]{2,0,1:T(8,128)(2,1)S(1)} all-to-all(bf16[16,160,1536]{2,0,1:T(8,128)(2,1)S(1)} %bitcast.152), channel_id=1, replica_groups=mesh['req'=8,'exp'=8,'hid'=4] {'exp','hid'}, dimensions={1} | all-to-all | bytes 15728640 | tf_op jit(solution)/shard_map/all_to_all | solution.py:218
  298.9 3.9 copy.114
  302.8 6.0 %convolution_bitcast_fusion.1 = f32[512,5,128]{2,0,1:T(8,128)S(1)} fusion(bf16[512,5,1536]{2,0,1:T(8,128)(2,1)} %bitcast.155, bf16[5,1536,128]{2,1,0:T(8,128)(2,1)} %param.35), kind=kOutput, calls=%fused_computation.23 | convolution fusion | flops 1006632960 | bytes 11141120 | tf_op jit(solution)/shard_map/red,edf->ref/dot_general | solution.py:52
  308.8 12.2 %convert_bitcast_fusion = bf16[512,5,1536]{2,0,1:T(8,128)(2,1)} fusion(bf16[5,128,1536]{2,1,0:T(8,128)(2,1)S(1)} %copy-done, bf16[512,5,1536]{2,0,1:T(8,128)(2,1)} %bitcast.156, bf16[5,1536,128]{2,1,0:T(8,128)(2,1)} %param.36, f32[512,5,128]{2,0,1:T(8,128)S(1)} %convolution_bitcast_fusion.1), kind=kOutput, calls=%fused_computation.7 | convolution fusion | flops 2019164160 | bytes 20971520 | tf_op jit(solution)/shard_map/ref,efd->red/dot_general | solution.py:59
  321.0 12.0 %copy.115 = bf16[512,5,1536]{2,1,0:T(8,128)(2,1)} copy(bf16[512,5,1536]{2,0,1:T(8,128)(2,1)} %convert_bitcast_fusion) | data formatting | bytes 15728640 | tf_op jit(solution)/shard_map/convert_element_type | solution.py:221
  332.9 5.2 all-to-all-start.1
  339.1 163.1 %all-to-all-done.1 = bf16[512,5,1536]{2,1,0:T(8,128)(2,1)} async-done(((bf16[512,5,1536]{2,1,0:T(8,128)(2,1)}), bf16[512,5,1536]{2,1,0:T(8,128)(2,1)}, u32[]{:S(2)}, u32[]{:S(2)}) %all-to-all-start.1) | async-done | bytes 7864352 | tf_op jit(solution)/shard_map/all_to_all | solution.py:222
  502.1 10.2 %reduce.1 = bf16[16,8,5,1536]{3,2,0,1:T(8,128)(2,1)} reduce(bf16[16,8,4,5,1536]{4,3,0,2,1:T(8,128)(2,1)} %bitcast.41, bf16[]{:T(256)} %constant.141.clone.1), dimensions={2}, to_apply=%region_15.16 | reduce | flops 2949120 | bytes 9830402 | tf_op jit(solution)/shard_map/reduce_sum | solution.py:224
  512.3 3.9 copy.117
  516.2 4.3 reshape.389
  520.5 5.4 %gather_fusion.1 = bf16[512,1536]{1,0:T(8,128)(2,1)S(1)} fusion(bf16[640,1536]{1,0:T(8,128)(2,1)} %reshape.389, s32[1024]{0:T(1024)S(1)} %pad_clamp_fusion), kind=kCustom, calls=%fused_computation.1 | custom fusion | bytes 3147776 | tf_op jit(solution)/shard_map/jit(_take)/gather | solution.py:226
  525.9 2.8 multiply_reduce_fusion
  (115 shorter events, 23.1 us)
Async XLA Ops:
  7.2 301.6 %copy-start = (bf16[5,128,1536]{2,1,0:T(8,128)(2,1)S(1)}, bf16[5,128,1536]{2,1,0:T(8,128)(2,1)}, u32[]{:S(2)}) copy-start(bf16[5,128,1536]{2,1,0:T(8,128)(2,1)} %param.37) | copy-start | bytes 5898244
  7.2 105.1 %all-reduce.2.cloned.1.call-start = ((), (), s32[]{:S(2)}) async-start(), calls=%async_computation.3 | async-start | bytes 917504 | tf_op jit(solution)/shard_map/psum | solution.py:120
  11.7 30.4 %copy-start.15 = (s32[8,4]{0,1:T(4,128)S(1)}, s32[8,4]{0,1:T(4,128)}, u32[]{:S(2)}) copy-start(s32[8,4]{0,1:T(4,128)} %param.30) | copy-start | bytes 388
  11.7 30.6 %copy-start.19 = (s32[64]{0:T(128)S(1)}, s32[64]{0:T(128)}, u32[]{:S(2)}) copy-start(s32[64]{0:T(128)} %param.31) | copy-start | bytes 772
  43.5 2.6 copy-start.20
  43.5 3.1 copy-start.3
  43.5 3.1 copy-start.17
  44.6 4.6 copy-start.16
  44.6 143.7 %reduce-scatter.2.cloned.1.call-start = ((), (), s32[]{:S(2)}) async-start(), calls=%async_computation.4 | async-start | bytes 983040 | tf_op jit(solution)/shard_map/reduce_scatter | solution.py:185
  51.2 0.6 copy-start.8
  51.2 0.6 copy-start.10
  123.1 3.4 copy-start.7
  123.1 3.9 copy-start.9
  123.1 3.9 copy-start.11
  123.1 3.9 copy-start.2
  127.0 7.8 %slice-start = ((bf16[4,57344]{1,0:T(4,128)(2,1)}), bf16[4,2048]{1,0:T(4,128)(2,1)S(1)}, s32[]{:S(2)}) async-start(bf16[4,57344]{1,0:T(4,128)(2,1)} %all-reduce.2.cloned.1.call-done), calls=%async_computation.5 | async-start | bytes 32768 | tf_op jit(solution)/shard_map/slice | solution.py:124
  127.1 8.0 %copy-start.4 = (bf16[256,1536]{1,0:T(8,128)(2,1)S(1)}, bf16[256,1536]{1,0:T(8,128)(2,1)}, u32[]{:S(2)}) copy-start(bf16[256,1536]{1,0:T(8,128)(2,1)} %param.19) | copy-start | bytes 2359300
  127.1 8.0 %copy-start.18 = (f32[1536]{0:T(1024)S(1)}, f32[1536]{0:T(1024)}, u32[]{:S(2)}) copy-start(f32[1536]{0:T(1024)} %param.20) | copy-start | bytes 18436
  152.6 8.2 %copy-start.1 = (f32[2,2048,256,3]{2,1,3,0:T(8,128)S(1)}, f32[2,2048,256,3]{2,1,3,0:T(8,128)}, u32[]{:S(2)}) copy-start(f32[2,2048,256,3]{2,1,3,0:T(8,128)} %get-tuple-element.17) | copy-start | bytes 37748740
  160.8 3.6 copy-start.6
  164.5 1.5 copy-start.12
  164.5 23.9 %copy-start.5 = (bf16[256,1536]{1,0:T(8,128)(2,1)S(1)}, bf16[256,1536]{1,0:T(8,128)(2,1)}, u32[]{:S(2)}) copy-start(bf16[256,1536]{1,0:T(8,128)(2,1)} %param.19) | copy-start | bytes 2359300
  164.5 25.0 %copy-start.13 = (f32[1536]{0:T(1024)S(1)}, f32[1536]{0:T(1024)}, u32[]{:S(2)}) copy-start(f32[1536]{0:T(1024)} %param.32) | copy-start | bytes 18436
  332.9 5.4 %copy-start.14 = (f32[64,8]{0,1:T(8,128)S(1)}, f32[64,8]{0,1:T(8,128)}, u32[]{:S(2)}) copy-start(f32[64,8]{0,1:T(8,128)} %param.34) | copy-start | bytes 6148
  332.9 169.2 %all-to-all-start.1 = ((bf16[512,5,1536]{2,1,0:T(8,128)(2,1)}), bf16[512,5,1536]{2,1,0:T(8,128)(2,1)}, u32[]{:S(2)}, u32[]{:S(2)}) async-start(bf16[512,5,1536]{2,1,0:T(8,128)(2,1)} %copy.115), calls=%async_computation.2 | async-start | bytes 25165824 | tf_op jit(solution)/shard_map/all_to_all | solution.py:222
Sparse Core Ops, SparseCore 0:
  44.7 67.4 all-reduce.1
  166.1 22.1 reduce-scatter.1
where the time goes:
time: 537 us; the launch traced here: 536 us
  waiting for transfers between devices  224 us (42%)
  blocking collectives  163 us (30%)
  local copies, waits for them, and re-layouts  57.7 us (11%)
  matrix products  42.8 us (8%)
  other arithmetic  28.6 us (5%)
  between operations  14.6 us (3%)
    all_to_all x1, waiting for transfers between devices, per_device(): lax.all_to_all(partials, ('exp', 'hid'), split_axis=0, concat_axis=1, til...  163 us
    all_to_all x1, blocking collectives, per_device(): lax.all_to_all(copies, ('exp', 'hid'), split_axis=1, concat_axis=0, tiled...  98.1 us
    psum x1, waiting for transfers between devices, per_device(): rows_pick = lax.psum(rows_pick, 'exp')  41.2 us
    all_gather x1, blocking collectives, per_device(): along_req = lax.all_gather(bank, 'req', axis=0, tiled=True)  29.4 us
    reduce_scatter x1, waiting for transfers between devices, per_device(): lax.psum_scatter(jnp.dot(attended, attention_output_weight, preferred_ele...  19.8 us
    all_gather x1, blocking collectives, per_device(): key_piece = lax.all_gather(keys_own, 'exp', axis=0, tiled=True)  19.2 us
    all_gather x1, blocking collectives, per_device(): value_piece = lax.all_gather(values_own, 'exp', axis=0, tiled=True)  15.9 us
    dot_general x1, matrix products, expert_rows(): jnp.einsum('ref,efd->red', hidden, expert_down_weight, preferred_element_...  12.2 us
  transfers between devices with their start and end apart: 3, of which 3 were waited for; matrix products, arithmetic and copies ran while one was open for 2% of the time, Pallas kernels for 0%

commit v1 on v0

--- a/solution.py
+++ b/solution.py
@@ -219,7 +219,15 @@
     partials = expert_rows(
         arrived, expert_gate_weight, expert_up_weight, expert_down_weight
     ).astype(jnp.bfloat16)
-    returned = lax.all_to_all(partials, ("exp", "hid"), split_axis=0, concat_axis=1, tiled=True)
+    returned = jnp.concatenate(
+        lax.all_to_all(
+            jnp.stack(jnp.split(partials, lax.axis_size(("exp", "hid")), axis=0)),
+            ("exp", "hid"),
+            0,
+            0,
+        ),
+        axis=1,
+    )
     returned = returned.reshape(capacity, exp_count, hid_count, local_exp, width)
     results = jnp.sum(returned.astype(jnp.float32), axis=2).astype(jnp.bfloat16)
     results = results.reshape(capacity * expert_count, width)

time: 537 us -> 506 us (0.942)
  waiting for transfers between devices: 224 us -> 151 us
  local copies, waits for them, and re-layouts: 57.7 us -> 98.6 us
    all_to_all x1, waiting for transfers between devices: 163 us -> 91.3 us  [per_device(): lax.all_to_all(jnp.stack(jnp.split(partials, lax.axis_size(('exp', 'hid')...]
    unnamed x51 -> x68, local copies, waits for them, and re-layouts: 7.44 us -> 58.3 us
    convert_element_type x1 -> x0, local copies, waits for them, and re-layouts: 12 us -> none  [per_device(): partials = expert_rows(arrived, expert_gate_weight, expert_up_weight, exp...]
where the time goes in v1:
time: 506 us; the launch traced here: 502 us
  blocking collectives  162 us (32%)
  waiting for transfers between devices  151 us (30%)
  local copies, waits for them, and re-layouts  98.6 us (19%)
  matrix products  45.4 us (9%)
  other arithmetic  25.3 us (5%)
  between operations  14.5 us (3%)
  starting transfers between devices  5.2 us (1%)
    all_to_all x1, blocking collectives, per_device(): lax.all_to_all(copies, ('exp', 'hid'), split_axis=1, concat_axis=0, tiled...  98.1 us
    all_to_all x1, waiting for transfers between devices, per_device(): lax.all_to_all(jnp.stack(jnp.split(partials, lax.axis_size(('exp', 'hid')...  91.3 us
    unnamed x68, local copies, waits for them, and re-layouts  58.3 us
    psum x1, waiting for transfers between devices, per_device(): rows_pick = lax.psum(rows_pick, 'exp')  39.7 us
    all_gather x1, blocking collectives, per_device(): along_req = lax.all_gather(bank, 'req', axis=0, tiled=True)  29.4 us
    reduce_scatter x1, waiting for transfers between devices, per_device(): lax.psum_scatter(jnp.dot(attended, attention_output_weight, preferred_ele...  19.8 us
    all_gather x1, blocking collectives, per_device(): key_piece = lax.all_gather(keys_own, 'exp', axis=0, tiled=True)  19.1 us
    all_gather x1, blocking collectives, per_device(): value_piece = lax.all_gather(values_own, 'exp', axis=0, tiled=True)  15.9 us
  transfers between devices with their start and end apart: 3, of which 3 were waited for; matrix products, arithmetic and copies ran while one was open for 2% of the time, Pallas kernels for 0%

profile of v1, /device:TPU:1, one launch (start us, length us, event | category | flops | bytes accessed | tf_op | source)
XLA Modules:
  0.0 502.1 jit_solution(15372367332503674267)
XLA Ops:
  11.7 29.4 %all-gather = bf16[8,1,57344]{2,1,0:T(2,128)(2,1)S(1)} all-gather(bf16[1,1,57344]{2,1,0:T(2,128)(2,1)S(1)} %maximum_bitcast_fusion), channel_id=1, replica_groups=mesh['req'=8,'exp'=8,'hid'=4] {'req'}, dimensions={0}, use_global_device_ids=true | all-gather | bytes 1032192 | tf_op jit(solution)/shard_map/all_gather | solution.py:114
  47.8 2.9 fusion.88
  50.7 1.7 fusion.90
  54.6 19.1 %all_gather.9 = bf16[2048,128]{0,1:T(8,128)(2,1)} all-gather(bf16[256,128]{0,1:T(8,128)(2,1)S(1)} %bitcast.284), channel_id=1, replica_groups=mesh['req'=8,'exp'=8,'hid'=4] {'exp'}, dimensions={0}, use_global_device_ids=true | all-gather | bytes 589824 | tf_op jit(solution)/shard_map/all_gather | solution.py:159
  73.7 39.7 %all-reduce.2.cloned.1.call-done = bf16[4,57344]{1,0:T(4,128)(2,1)} async-done(((bf16[4,57344]{1,0:T(4,128)(2,1)}), bf16[4,57344]{1,0:T(4,128)(2,1)}) %all-reduce.2.cloned.1.call-update) | async-done | bytes 458768 | tf_op jit(solution)/shard_map/psum | solution.py:120
  113.3 1.9 fusion.92
  115.2 2.1 reshape.380
  118.6 2.2 fusion.86
  120.8 2.1 reshape.382
  129.8 7.9 %fusion = (f32[2,3,256]{2,1,0:T(4,128)S(1)}, f32[2,2048,256,3]{2,1,3,0:T(8,128)}) fusion(pred[256,2048]{0,1:T(8,128)(4,1)} %fusion.6, bf16[2048,2,64,1]{0,2,3,1:T(8,128)(2,1)} %bitcast.282, bf16[256,2,3,32]{0,3,2,1:T(8,128)(2,1)S(1)} %bitcast.293, bf16[256,2,3,32]{0,3,2,1:T(8,128)(2,1)S(1)} %bitcast.292), kind=kOutput, calls=%fused_computation.4 | convolution fusion | flops 412482048 | bytes 13834240 | tf_op jit(solution)/shard_map/qkgh,nkh->kgqn/dot_general | solution.py:168
  139.3 15.9 %all_gather.11 = bf16[2048,128]{1,0:T(8,128)(2,1)S(1)} all-gather(bf16[256,128]{1,0:T(8,128)(2,1)S(1)} %fusion.21), channel_id=1, replica_groups=mesh['req'=8,'exp'=8,'hid'=4] {'exp'}, dimensions={0}, use_global_device_ids=true | all-gather | bytes 589824 | tf_op jit(solution)/shard_map/all_gather | solution.py:160
  156.3 7.5 %fusion.1 = f32[2,3,256]{2,1,0:T(4,128)S(1)} fusion(f32[2,2048,256,3]{2,1,3,0:T(8,128)} %get-tuple-element.17, f32[2,3,256]{2,1,0:T(4,128)S(1)} %broadcast_maximum_fusion, pred[256,2048]{0,1:T(8,128)(4,1)S(1)} %copy-done.2), kind=kLoop, calls=%fused_computation.5 | loop fusion | flops 15727104 | bytes 13119488 | tf_op jit(solution)/shard_map/reduce_sum | solution.py:174
  164.6 3.6 fusion.25
  172.3 19.8 %reduce-scatter.2.cloned.1.call-done = bf16[64,1536]{1,0:T(8,128)(2,1)} async-done(((bf16[256,1536]{1,0:T(8,128)(2,1)}), bf16[64,1536]{1,0:T(8,128)(2,1)}) %reduce-scatter.2.cloned.1.call-update) | async-done | bytes 196624 | tf_op jit(solution)/shard_map/reduce_scatter | solution.py:185
  193.2 3.0 convolution_convert_fusion
  196.2 4.3 broadcast_in_dim.153
  200.5 3.2 copy.107
  204.6 98.1 %all_to_all.23 = bf16[16,160,1536]{2,0,1:T(8,128)(2,1)S(1)} all-to-all(bf16[16,160,1536]{2,0,1:T(8,128)(2,1)S(1)} %bitcast.276), channel_id=1, replica_groups=mesh['req'=8,'exp'=8,'hid'=4] {'exp','hid'}, dimensions={1} | all-to-all | bytes 15728640 | tf_op jit(solution)/shard_map/all_to_all | solution.py:218
  302.7 3.9 copy.108
  306.5 6.0 %convolution_bitcast_fusion.1 = f32[512,5,128]{2,0,1:T(8,128)S(1)} fusion(bf16[512,5,1536]{2,0,1:T(8,128)(2,1)} %bitcast.279, bf16[5,1536,128]{2,1,0:T(8,128)(2,1)} %param.35), kind=kOutput, calls=%fused_computation.24 | convolution fusion | flops 1006632960 | bytes 11141120 | tf_op jit(solution)/shard_map/red,edf->ref/dot_general | solution.py:52
  312.5 12.2 %convert_bitcast_fusion = bf16[512,5,1536]{2,0,1:T(8,128)(2,1)} fusion(bf16[5,128,1536]{2,1,0:T(8,128)(2,1)S(1)} %copy-done, bf16[512,5,1536]{2,0,1:T(8,128)(2,1)} %bitcast.280, bf16[5,1536,128]{2,1,0:T(8,128)(2,1)} %param.36, f32[512,5,128]{2,0,1:T(8,128)S(1)} %convolution_bitcast_fusion.1), kind=kOutput, calls=%fused_computation.8 | convolution fusion | flops 2019164160 | bytes 20971520 | tf_op jit(solution)/shard_map/ref,efd->red/dot_general | solution.py:59
  328.0 1.7 fusion.58
  329.7 1.7 fusion.57
  333.0 1.7 fusion.55
  346.3 1.7 fusion.47
  377.8 5.1 %all-to-all-start.1 = ((bf16[32,16,5,1536]{3,1,2,0:T(8,128)(2,1)}), bf16[32,16,5,1536]{3,1,2,0:T(8,128)(2,1)}, u32[]{:S(2)}, u32[]{:S(2)}) async-start(bf16[32,16,5,1536]{3,1,2,0:T(8,128)(2,1)} %fusion.29), calls=%async_computation.2 | async-start | bytes 15728640 | tf_op jit(solution)/shard_map/all_to_all | solution.py:223
  383.8 91.3 %all-to-all-done.1 = bf16[32,16,5,1536]{3,1,2,0:T(8,128)(2,1)} async-done(((bf16[32,16,5,1536]{3,1,2,0:T(8,128)(2,1)}), bf16[32,16,5,1536]{3,1,2,0:T(8,128)(2,1)}, u32[]{:S(2)}, u32[]{:S(2)}) %all-to-all-start.1) | async-done | bytes 7864352 | tf_op jit(solution)/shard_map/all_to_all | solution.py:223
  475.1 4.9 bitcast_reduce_fusion
  480.0 2.8 copy.109
  482.8 4.3 reshape.388
  487.1 5.4 %gather_fusion.1 = bf16[512,1536]{1,0:T(8,128)(2,1)S(1)} fusion(bf16[640,1536]{1,0:T(8,128)(2,1)} %reshape.388, s32[1024]{0:T(1024)S(1)} %pad_clamp_fusion), kind=kCustom, calls=%fused_computation.1 | custom fusion | bytes 3147776 | tf_op jit(solution)/shard_map/jit(_take)/gather | solution.py:234
  492.5 2.8 multiply_reduce_fusion
  (132 shorter events, 78.3 us)
Async XLA Ops:
  7.2 305.3 %copy-start = (bf16[5,128,1536]{2,1,0:T(8,128)(2,1)S(1)}, bf16[5,128,1536]{2,1,0:T(8,128)(2,1)}, u32[]{:S(2)}) copy-start(bf16[5,128,1536]{2,1,0:T(8,128)(2,1)} %param.37) | copy-start | bytes 5898244
  7.2 40.2 %copy-start.13 = (s32[1,4]{1,0:T(1,128)S(1)}, s32[1,4]{1,0:T(1,128)}, u32[]{:S(2)}) copy-start(s32[1,4]{1,0:T(1,128)} %param.29) | copy-start | bytes 52
  7.2 40.7 %copy-start.12 = (f32[1536]{0:T(1024)S(1)}, f32[1536]{0:T(1024)}, u32[]{:S(2)}) copy-start(f32[1536]{0:T(1024)} %param.20) | copy-start | bytes 18436
  7.2 106.1 %all-reduce.2.cloned.1.call-start = ((), (), s32[]{:S(2)}) async-start(), calls=%async_computation.3 | async-start | bytes 917504 | tf_op jit(solution)/shard_map/psum | solution.py:120
  45.9 146.2 %reduce-scatter.2.cloned.1.call-start = ((), (), s32[]{:S(2)}) async-start(), calls=%async_computation.4 | async-start | bytes 983040 | tf_op jit(solution)/shard_map/reduce_scatter | solution.py:185
  53.9 0.6 copy-start.7
  53.9 0.6 copy-start.8
  128.7 9.0 %slice-start = ((bf16[4,57344]{1,0:T(4,128)(2,1)}), bf16[4,2048]{1,0:T(4,128)(2,1)S(1)}, s32[]{:S(2)}) async-start(bf16[4,57344]{1,0:T(4,128)(2,1)} %all-reduce.2.cloned.1.call-done), calls=%async_computation.5 | async-start | bytes 32768 | tf_op jit(solution)/shard_map/slice | solution.py:124
  128.9 9.0 %copy-start.3 = (bf16[256,1536]{1,0:T(8,128)(2,1)S(1)}, bf16[256,1536]{1,0:T(8,128)(2,1)}, u32[]{:S(2)}) copy-start(bf16[256,1536]{1,0:T(8,128)(2,1)} %param.19) | copy-start | bytes 2359300
  129.8 26.5 %copy-start.2 = (pred[256,2048]{0,1:T(8,128)(4,1)S(1)}, pred[256,2048]{0,1:T(8,128)(4,1)}, u32[]{:S(2)}) copy-start(pred[256,2048]{0,1:T(8,128)(4,1)} %fusion.6) | copy-start | bytes 1572868
  156.3 8.2 %copy-start.1 = (f32[2,2048,256,3]{2,1,3,0:T(8,128)S(1)}, f32[2,2048,256,3]{2,1,3,0:T(8,128)}, u32[]{:S(2)}) copy-start(f32[2,2048,256,3]{2,1,3,0:T(8,128)} %get-tuple-element.17) | copy-start | bytes 37748740
  156.3 8.3 %copy-start.6 = (bf16[2048,128]{0,1:T(8,128)(2,1)S(1)}, bf16[2048,128]{0,1:T(8,128)(2,1)}, u32[]{:S(2)}) copy-start(bf16[2048,128]{0,1:T(8,128)(2,1)} %copy.98) | copy-start | bytes 1572868
  164.6 3.6 copy-start.5
  164.6 5.1 %copy-start.9 = (s32[64,8]{0,1:T(8,128)S(1)}, s32[64,8]{0,1:T(8,128)}, u32[]{:S(2)}) copy-start(s32[64,8]{0,1:T(8,128)} %param.33) | copy-start | bytes 6148
  164.6 27.5 %copy-start.4 = (bf16[256,1536]{1,0:T(8,128)(2,1)S(1)}, bf16[256,1536]{1,0:T(8,128)(2,1)}, u32[]{:S(2)}) copy-start(bf16[256,1536]{1,0:T(8,128)(2,1)} %param.19) | copy-start | bytes 2359300
  164.6 28.6 %copy-start.10 = (f32[1536]{0:T(1024)S(1)}, f32[1536]{0:T(1024)}, u32[]{:S(2)}) copy-start(f32[1536]{0:T(1024)} %param.32) | copy-start | bytes 18436
  377.8 5.3 %copy-start.11 = (f32[64,8]{0,1:T(8,128)S(1)}, f32[64,8]{0,1:T(8,128)}, u32[]{:S(2)}) copy-start(f32[64,8]{0,1:T(8,128)} %param.34) | copy-start | bytes 6148
  377.8 97.3 %all-to-all-start.1 = ((bf16[32,16,5,1536]{3,1,2,0:T(8,128)(2,1)}), bf16[32,16,5,1536]{3,1,2,0:T(8,128)(2,1)}, u32[]{:S(2)}, u32[]{:S(2)}) async-start(bf16[32,16,5,1536]{3,1,2,0:T(8,128)(2,1)} %fusion.29), calls=%async_computation.2 | async-start | bytes 15728640 | tf_op jit(solution)/shard_map/all_to_all | solution.py:223
Sparse Core Ops, SparseCore 0:
  46.0 67.2 all-reduce.1
  169.8 22.1 reduce-scatter.1
